TPU v7x, 512 devices: a whole 4x4x16 slice. The times are simulated.
512 devices in a mesh: band: 16 (over x, y), lon: 32 (over z, core).
Axes of the slice: x: 4, y: 4, z: 16, core: 2. Of those that a mesh axis runs over, the one named last changes fastest.
Arguments:
- sky_maps: float32 [16, 8192, 256], P(None, ('band', 'lon')), may hold values from -9 to 9
- noise_var: float32 [8192, 256], P(('band', 'lon')), may hold values from 1 to 4
- position: float32 [3, 8192, 256], P(None, ('band', 'lon')), may hold values from -1 to 1
- leaf_basis: float32 [8192, 256, 64], P(('band', 'lon')), may hold values from -1 to 1
- leaf_couple: float32 [8192, 4, 64, 64], P(('band', 'lon')), as said below
- transfer: float32 [8192, 64, 64], P(('band', 'lon')), may hold values from -2 to 2
- panel_couple: float32 [1024, 2, 64, 64], P(('band', 'lon')), as said below
- near_list: int32 [8192, 5], P(('band', 'lon')), may hold values from -1 to 8191, as said below
- far_list: int32 [8192, 4], P(('band', 'lon')), may hold values from 0 to 8191, as said below
- panel_list: int32 [1024, 2], P(('band', 'lon')), may hold values from 0 to 1023, as said below
- leaf_panel: int32 [8192], P(('band', 'lon')), may hold values from 0 to 1
Outputs:
- solution: float32 [16, 8192, 256], P(None, ('band', 'lon'))
- residual: float32 [16, 8192, 256], P(None, ('band', 'lon'))
Inputs may be any that keep to these rules, and one draw needn't show every extreme that they name: `near_list`: entry 0 of a row is the leaf itself; the entries after it that are not -1 come first and are distinct leaves of the same band at cycle distance 1 or 2, the cycle closing; leaf j stands in leaf i's row exactly when i stands in j's. `far_list`: distinct leaves of the same band at cycle distance 3 to 6, the cycle closing; leaf j stands in leaf i's row exactly when i stands in j's. If leaf j stands in slot s of far_list[i] and leaf i in slot t of far_list[j], then leaf_couple[j, t] is the transpose of leaf_couple[i, s]. `panel_list`: entries are panel s of sectors of other bands at the same longitude (sector ids differing by a nonzero multiple of the sectors of a band), s being the panel's own index in its sector; panel j stands in panel k's row as often as k stands in j's. If panel j stands in slot s of panel_list[k] and these slots pair up with the slots t of panel_list[j] that hold k, then panel_couple[j, t] is the transpose of panel_couple[k, s].
All inputs are finite; a program needn't handle non-finite values.
Results may differ from a plain program's by a relative error of at most 0.0003.
Values sent between devices are 32-bit elements; how exact they have to be, the bound alone decides.
No kernel may reach another device: no remote copies, remote signals or barrier semaphores. Data moves between devices by JAX's collectives and lax.ppermute only.
A program may use at most 128 MiB of HBM per device.

v0:
```python
import math
import jax
import jax.numpy as jnp
from jax import lax
from jax.sharding import PartitionSpec as P

REACH = 6
ITERS = 2
HIGHEST_PRECISION = lax.Precision.HIGHEST
ROOT_THREE = math.sqrt(3.0)
AMPLITUDE = 0.02


def extended(cells, sides, width):
    for axis, dim in sides:
        count = lax.axis_size(axis)
        head = lax.slice_in_dim(cells, 0, width, axis=dim)
        tail = lax.slice_in_dim(cells, cells.shape[dim] - width, cells.shape[dim], axis=dim)
        cells = jnp.concatenate(
            [
                lax.ppermute(tail, axis, [(i, (i + 1) % count) for i in range(count)]),
                cells,
                lax.ppermute(head, axis, [((i + 1) % count, i) for i in range(count)]),
            ],
            axis=dim,
        )
    return cells


def matern_block(rows_pos, cols_pos, length_scale):
    squared = jnp.zeros((cols_pos.shape[1], rows_pos.shape[1], cols_pos.shape[2]), jnp.float32)
    for component in range(3):
        offset = rows_pos[component][None, :, None] - cols_pos[component][:, None, :]
        squared = squared + offset * offset
    scaled = ROOT_THREE * jnp.sqrt(squared) / length_scale
    return AMPLITUDE * (1.0 + scaled) * jnp.exp(-scaled)


def on_device(
    sky_maps,
    noise_var,
    position,
    leaf_basis,
    leaf_couple,
    transfer,
    panel_couple,
    near_list,
    far_list,
    panel_list,
    leaf_panel,
):
    lon_index = lax.axis_index("lon")
    lon_count = lax.axis_size("lon")
    local_leaves = sky_maps.shape[1]
    pixel_count = sky_maps.shape[2]
    cycle_size = local_leaves * lon_count
    panel_count = panel_couple.shape[0]
    length_scale = 2.0 * math.pi / cycle_size
    first_leaf = lon_index * local_leaves
    near_depth = 2

    def rim_index(leaf_ids, depth):
        return (leaf_ids % cycle_size - first_leaf + depth) % cycle_size

    near_valid = near_list >= 0
    near_rows = rim_index(jnp.where(near_valid, near_list, near_list[:, :1]), near_depth)
    far_rows = rim_index(far_list, REACH)
    rim_pos = extended(position, (("lon", 1),), near_depth)

    def leaf_blocks(inputs):
        rows_pos, rows_index, slot_mask = inputs
        cols_pos = rim_pos[:, rows_index]
        return matern_block(rows_pos, cols_pos, length_scale) * slot_mask[:, None, None]

    near_blocks = lax.map(
        leaf_blocks, (jnp.transpose(position, (1, 0, 2)), near_rows, near_valid.astype(jnp.float32))
    )
    band_slot = panel_list // (lon_count * panel_count)
    gathered_rows = band_slot * panel_count + panel_list % panel_count
    membership = (leaf_panel[:, None] == jnp.arange(panel_count, dtype=jnp.int32)[None, :]).astype(
        jnp.float32
    )

    def square_total(vector):
        return lax.psum(jnp.sum(vector * vector, axis=(1, 2)), ("band", "lon"))

    solution = jnp.zeros_like(sky_maps)
    residual = sky_maps
    direction = sky_maps
    norm_now = square_total(residual)
    for iteration in range(ITERS):
        coeffs = jnp.einsum("lpr,mlp->mlr", leaf_basis, direction, precision=HIGHEST_PRECISION)
        joined = jnp.concatenate([direction, coeffs], axis=2)
        rim_joined = extended(joined, (("lon", 1),), REACH)
        rim_values = rim_joined[
            :, REACH - near_depth : REACH + local_leaves + near_depth, :pixel_count
        ]
        rim_coeffs = rim_joined[:, :, pixel_count:]
        near_part = jnp.einsum(
            "lspq,mlsq->mlp", near_blocks, rim_values[:, near_rows], precision=HIGHEST_PRECISION
        )
        leaf_far = jnp.einsum(
            "lsab,mlsb->mla", leaf_couple, rim_coeffs[:, far_rows], precision=HIGHEST_PRECISION
        )
        upward = jnp.einsum("lab,mla->mlb", transfer, coeffs, precision=HIGHEST_PRECISION)
        panel_coeffs = jnp.einsum("lk,mlb->mkb", membership, upward, precision=HIGHEST_PRECISION)
        band_coeffs = lax.all_gather(panel_coeffs, "band", axis=1, tiled=True)
        panel_far = jnp.einsum(
            "ksab,mksb->mka",
            panel_couple,
            band_coeffs[:, gathered_rows],
            precision=HIGHEST_PRECISION,
        )
        downward = jnp.einsum("lk,mkb->mlb", membership, panel_far, precision=HIGHEST_PRECISION)
        leaf_far = leaf_far + jnp.einsum(
            "lab,mlb->mla", transfer, downward, precision=HIGHEST_PRECISION
        )
        far_part = jnp.einsum("lpr,mlr->mlp", leaf_basis, leaf_far, precision=HIGHEST_PRECISION)
        applied = noise_var[None] * direction + near_part + far_part
        curvature_sum = lax.psum(jnp.sum(direction * applied, axis=(1, 2)), ("band", "lon"))
        step_size = norm_now / curvature_sum
        solution = solution + step_size[:, None, None] * direction
        residual = residual - step_size[:, None, None] * applied
        if iteration + 1 < ITERS:
            norm_next = square_total(residual)
            direction = residual + (norm_next / norm_now)[:, None, None] * direction
            norm_now = norm_next
    return (solution, residual)


def solution(mesh):
    placed = (
        P(None, ("band", "lon"), None),
        P(("band", "lon"), None),
        P(None, ("band", "lon"), None),
        P(("band", "lon"), None, None),
        P(("band", "lon"), None, None, None),
        P(("band", "lon"), None, None),
        P(("band", "lon"), None, None, None),
        P(("band", "lon"), None),
        P(("band", "lon"), None),
        P(("band", "lon"), None),
        P(("band", "lon")),
    )
    return jax.shard_map(
        on_device,
        mesh=mesh,
        in_specs=placed,
        out_specs=(P(None, ("band", "lon"), None), P(None, ("band", "lon"), None)),
        check_vma=False,
    )
```

profile of v0, /device:TPU:1, one launch (start us, length us, event | category | flops | bytes accessed | tf_op | source)
XLA Modules:
  0.0 555.7 jit_solution(6584740147777887504)
XLA Ops:
  1.7 3.0 collective-permute-start.2
  4.7 4.4 collective-permute-start.3
  13.5 3.6 collective-permute-start.1
  20.4 20.6 %all_gather.6 = f32[16,32,64]{2,0,1:T(8,128)} all-gather(f32[16,2,64]{2,0,1:T(8,128)S(1)} %copy.56), channel_id=1, replica_groups=mesh['band'=16,'lon'=32] {'band'}, dimensions={1}, use_global_device_ids=true | all-gather | bytes 139264 | tf_op jit(solution)/shard_map/all_gather | solution.py:107
  46.6 98.0 %while.12 = (s32[]{:T(128)}, f32[16,5,256,256]{3,2,1,0:T(8,128)}, f32[16,3,256]{2,1,0:T(4,128)}, s32[16,5]{1,0:T(8,128)S(1)}, f32[3,20,256]{2,0,1:T(4,128)S(1)},...) while((s32[]{:T(128)}, f32[16,5,256,256]{3,2,1,0:T(8,128)}, f32[16,3,256]{2,1,0:T(4,128)}, ...), condition=%wide.region_3.4_spmd, body=%wide.region_2.3_spmd.sunk | while | flops 4588563 | bytes 1434957 | solution.py:75
  50.1 2.8 multiply_dynamic-update-slice_fusion.2
  62.3 2.8 multiply_dynamic-update-slice_fusion.2
  68.4 2.8 multiply_dynamic-update-slice_fusion.2
  74.5 2.8 multiply_dynamic-update-slice_fusion.2
  80.6 2.8 multiply_dynamic-update-slice_fusion.2
  86.7 2.9 multiply_dynamic-update-slice_fusion.2
  92.9 2.8 multiply_dynamic-update-slice_fusion.2
  105.1 2.9 multiply_dynamic-update-slice_fusion.2
  117.3 2.8 multiply_dynamic-update-slice_fusion.2
  129.6 2.9 multiply_dynamic-update-slice_fusion.2
  148.7 2.9 convolution_bitcast_fusion.9
  155.8 21.5 %fusion.6 = f32[16,16,256]{2,0,1:T(8,128)S(1)} fusion(f32[16,16,5,256]{3,0,2,1:T(8,128)} %bitcast.154, f32[16,5,256,256]{3,2,1,0:T(8,128)} %get-tuple-element.79, f32[16,256]{1,0:T(8,128)S(1)} %copy-done.23, f32[16,16,256]{2,1,0:T(8,128)S(1)} %copy-done.1), kind=kOutput, calls=%fused_computation.28 | convolution fusion | flops 1006764032 | bytes 22822912 | tf_op jit(solution)/shard_map/lspq,mlsq->mlp/dot_general | solution.py:99
  178.1 107.3 %all-reduce = (f32[16]{0:T(128)S(1)}, f32[16]{0:T(128)S(1)}) all-reduce(f32[16]{0:T(128)S(1)} %copy-done.33, f32[16]{0:T(128)S(1)} %get-tuple-element.120), channel_id=1, replica_groups=mesh['band'=16,'lon'=32] {'band','lon'}, use_global_device_ids=true, to_apply=%region_1.2 | all-reduce | flops 32 | bytes 256 | tf_op jit(solution)/shard_map/psum | solution.py:85
  285.7 100.1 %psum.30 = f32[16]{0:T(128)S(1)} all-reduce(f32[16]{0:T(128)S(1)} %multiply_reduce_fusion.1), channel_id=1, replica_groups=mesh['band'=16,'lon'=32] {'band','lon'}, use_global_device_ids=true, to_apply=%region_7.8 | all-reduce | flops 16 | bytes 128 | tf_op jit(solution)/shard_map/psum | solution.py:85
  389.8 17.5 %all_gather.7 = f32[16,32,64]{2,0,1:T(8,128)S(1)} all-gather(f32[16,2,64]{2,0,1:T(8,128)S(1)} %copy.64), channel_id=1, replica_groups=mesh['band'=16,'lon'=32] {'band'}, dimensions={1}, use_global_device_ids=true | all-gather | bytes 139264 | tf_op jit(solution)/shard_map/all_gather | solution.py:107
  409.1 5.9 %collective-permute-start.4 = (f32[16,6,320]{2,0,1:T(8,128)}, f32[16,6,320]{2,0,1:T(8,128)S(1)}, u32[]{:S(2)}, u32[]{:S(2)}) collective-permute-start(f32[16,6,320]{2,0,1:T(8,128)} %get-tuple-element.110), channel_id=1, source_target_pairs={{0,1},{1,2},{2,3},{3,4},{4,5},{5,6},{6,7},{7,8},{8,9},{9,10},{10,1... | collective-permute-start | bytes 368648 | tf_op jit(solution)/shard_map/ppermute | solution.py:21
  423.2 3.6 convolution_bitcast_fusion.6
  428.6 21.5 %fusion.5 = f32[16,16,256]{2,0,1:T(8,128)S(1)} fusion(f32[16,16,5,256]{3,0,2,1:T(8,128)} %bitcast.153, f32[16,5,256,256]{3,2,1,0:T(8,128)} %get-tuple-element.79, f32[16,16,256]{2,0,1:T(8,128)S(1)} %multiply_add_fusion.1, f32[16,256]{1,0:T(8,128)S(1)} %copy-done.23), kind=kOutput, calls=%fused_computation.26 | convolution fusion | flops 1006764032 | bytes 22822912 | tf_op jit(solution)/shard_map/lspq,mlsq->mlp/dot_general | solution.py:99
  451.8 102.0 %psum.31 = f32[16]{0:T(128)S(1)} all-reduce(f32[16]{0:T(128)S(1)} %get-tuple-element.122), channel_id=1, replica_groups=mesh['band'=16,'lon'=32] {'band','lon'}, use_global_device_ids=true, to_apply=%region_9.10 | all-reduce | flops 16 | bytes 128 | tf_op jit(solution)/shard_map/psum | solution.py:120
  (325 shorter events, 111.7 us)
Async XLA Ops:
  0.6 148.0 %copy-start = (f32[16,4,64,64]{3,2,1,0:T(8,128)S(1)}, f32[16,4,64,64]{3,2,1,0:T(8,128)}, u32[]{:S(2)}) copy-start(f32[16,4,64,64]{3,2,1,0:T(8,128)} %param.17) | copy-start | bytes 3145732
  1.7 43.5 %collective-permute-start.2 = (f32[3,2,256]{2,0,1:T(4,128)S(1)}, f32[3,2,256]{2,0,1:T(4,128)S(1)}, u32[]{:S(2)}, u32[]{:S(2)}) collective-permute-start(f32[3,2,256]{2,0,1:T(4,128)S(1)} %get-tuple-element.116), channel_id=1, source_target_pairs={{0,1},{1,2},{2,3},{3,4},{4,5},{5,6},{6,7},{7,8},{8,9},{9,10},{10,1... | collective-permute-start | bytes 18440 | tf_op jit(solution)/shard_map/ppermute | solution.py:21
  4.7 12.3 %copy-start.1 = (f32[16,16,256]{2,1,0:T(8,128)S(1)}, f32[16,16,256]{2,1,0:T(8,128)}, u32[]{:S(2)}) copy-start(f32[16,16,256]{2,1,0:T(8,128)} %param.13) | copy-start | bytes 786436
  4.7 41.0 %collective-permute-start.3 = (f32[3,2,256]{2,0,1:T(4,128)S(1)}, f32[3,2,256]{2,0,1:T(4,128)}, u32[]{:S(2)}, u32[]{:S(2)}) collective-permute-start(f32[3,2,256]{2,0,1:T(4,128)S(1)} %get-tuple-element.117), channel_id=1, source_target_pairs={{1,0},{2,1},{3,2},{4,3},{5,4},{6,5},{7,6},{8,7},{9,8},{10,9},{11,1... | collective-permute-start | bytes 18440 | tf_op jit(solution)/shard_map/ppermute | solution.py:23
  10.2 7.6 %copy-start.30 = (s32[16,5]{0,1:T(8,128)S(1)}, s32[16,5]{0,1:T(8,128)}, u32[]{:S(2)}) copy-start(s32[16,5]{0,1:T(8,128)} %param.20) | copy-start | bytes 964
  10.3 7.7 %copy-start.32 = (s32[2,2]{1,0:T(2,128)S(1)}, s32[2,2]{1,0:T(2,128)}, u32[]{:S(2)}) copy-start(s32[2,2]{1,0:T(2,128)} %param.22) | copy-start | bytes 52
  10.3 7.8 %copy-start.31 = (s32[16,4]{0,1:T(4,128)S(1)}, s32[16,4]{0,1:T(4,128)}, u32[]{:S(2)}) copy-start(s32[16,4]{0,1:T(4,128)} %param.21) | copy-start | bytes 772
  10.3 9.4 %copy-start.4 = (f32[16,64,64]{2,1,0:T(8,128)S(1)}, f32[16,64,64]{2,1,0:T(8,128)}, u32[]{:S(2)}) copy-start(f32[16,64,64]{2,1,0:T(8,128)} %param.18) | copy-start | bytes 786436
  10.3 9.9 %copy-start.25 = (s32[16]{0:T(128)S(1)}, s32[16]{0:T(128)}, u32[]{:S(2)}) copy-start(s32[16]{0:T(128)} %param.23) | copy-start | bytes 196
  12.7 131.9 %copy-start.7 = (f32[16,16,64]{2,0,1:T(8,128)}, f32[16,16,64]{2,0,1:T(8,128)S(1)}, u32[]{:S(2)}) copy-start(f32[16,16,64]{2,0,1:T(8,128)S(1)} %convolution_bitcast_fusion.11) | copy-start | bytes 196612
  13.5 131.1 %collective-permute-start = (f32[16,6,320]{2,0,1:T(8,128)}, f32[16,6,320]{2,0,1:T(8,128)S(1)}, u32[]{:S(2)}, u32[]{:S(2)}) collective-permute-start(f32[16,6,320]{2,0,1:T(8,128)} %get-tuple-element.112), channel_id=1, source_target_pairs={{0,1},{1,2},{2,3},{3,4},{4,5},{5,6},{6,7},{7,8},{8,9},{9,10},{10,1... | collective-permute-start | bytes 368648 | tf_op jit(solution)/shard_map/ppermute | solution.py:21
  13.5 131.1 %collective-permute-start.1 = (f32[16,6,320]{2,0,1:T(8,128)}, f32[16,6,320]{2,0,1:T(8,128)}, u32[]{:S(2)}, u32[]{:S(2)}) collective-permute-start(f32[16,6,320]{2,0,1:T(8,128)} %get-tuple-element.113), channel_id=1, source_target_pairs={{1,0},{2,1},{3,2},{4,3},{5,4},{6,5},{7,6},{8,7},{9,8},{10,9},{11,1... | collective-permute-start | bytes 368648 | tf_op jit(solution)/shard_map/ppermute | solution.py:23
  18.0 28.6 %copy-start.24 = (s32[1024]{0:T(1024)}, s32[1024]{0:T(1024)S(1)}, u32[]{:S(2)}) copy-start(s32[1024]{0:T(1024)S(1)} %pad_clamp_fusion.1) | copy-start | bytes 12292
  144.6 6.9 %copy-start.11 = (f32[16,6,320]{2,0,1:T(8,128)}, f32[16,6,320]{2,0,1:T(8,128)S(1)}, u32[]{:S(2)}) copy-start(f32[16,6,320]{2,0,1:T(8,128)S(1)} %collective-permute-done) | copy-start | bytes 368644
  155.8 21.5 %copy-start.2 = (f32[16,256,64]{1,2,0:T(8,128)S(1)}, f32[16,256,64]{1,2,0:T(8,128)}, u32[]{:S(2)}) copy-start(f32[16,256,64]{1,2,0:T(8,128)} %param.16) | copy-start | bytes 3145732
  155.8 21.5 %copy-start.16 = (f32[16,16,64]{2,0,1:T(8,128)S(1)}, f32[16,16,64]{2,0,1:T(8,128)}, u32[]{:S(2)}) copy-start(f32[16,16,64]{2,0,1:T(8,128)} %fusion.8) | copy-start | bytes 196612
  178.1 210.1 %copy-start.5 = (f32[16,16,256]{2,0,1:T(8,128)}, f32[16,16,256]{2,0,1:T(8,128)S(1)}, u32[]{:S(2)}) copy-start(f32[16,16,256]{2,0,1:T(8,128)S(1)} %get-tuple-element.121) | copy-start | bytes 786436
  388.9 32.8 %copy-start.21 = (s32[1024]{0:T(1024)S(1)}, s32[1024]{0:T(1024)}, u32[]{:S(2)}) copy-start(s32[1024]{0:T(1024)} %pad_clamp_fusion.2) | copy-start | bytes 12292
  409.1 8.3 %collective-permute-start.4 = (f32[16,6,320]{2,0,1:T(8,128)}, f32[16,6,320]{2,0,1:T(8,128)S(1)}, u32[]{:S(2)}, u32[]{:S(2)}) collective-permute-start(f32[16,6,320]{2,0,1:T(8,128)} %get-tuple-element.110), channel_id=1, source_target_pairs={{0,1},{1,2},{2,3},{3,4},{4,5},{5,6},{6,7},{7,8},{8,9},{9,10},{10,1... | collective-permute-start | bytes 368648 | tf_op jit(solution)/shard_map/ppermute | solution.py:21
  415.0 5.1 collective-permute-start.5
  428.6 21.5 %copy-start.18 = (f32[16,16,64]{2,1,0:T(8,128)S(1)}, f32[16,16,64]{2,1,0:T(8,128)}, u32[]{:S(2)}) copy-start(f32[16,16,64]{2,1,0:T(8,128)} %convolution_bitcast_fusion.4) | copy-start | bytes 196612
  428.6 21.5 %copy-start.19 = (f32[16,16,64]{2,1,0:T(8,128)S(1)}, f32[16,16,64]{2,1,0:T(8,128)}, u32[]{:S(2)}) copy-start(f32[16,16,64]{2,1,0:T(8,128)} %convolution_bitcast_fusion.6) | copy-start | bytes 196612
  428.6 22.4 %copy-start.3 = (f32[16,256,64]{1,2,0:T(8,128)S(1)}, f32[16,256,64]{1,2,0:T(8,128)}, u32[]{:S(2)}) copy-start(f32[16,256,64]{1,2,0:T(8,128)} %param.16) | copy-start | bytes 3145732
  450.1 103.7 %copy-start.6 = (f32[16,16,256]{2,0,1:T(8,128)S(1)}, f32[16,16,256]{2,0,1:T(8,128)}, u32[]{:S(2)}) copy-start(f32[16,16,256]{2,0,1:T(8,128)} %copy-done.5) | copy-start | bytes 786436
  (46 other events, 131.6 us)
where the time goes:
time: 558 us; the launch traced here: 556 us
  blocking collectives  347 us (62%)
  local copies, waits for them, and re-layouts  67.1 us (12%)
  matrix products  63.6 us (11%)
  other arithmetic  54.6 us (10%)
  starting transfers between devices  16.9 us (3%)
    psum x2, blocking collectives, square_total(): return lax.psum(jnp.sum(vector * vector, axis=(1, 2)), ('band', 'lon'))  207 us
    psum x1, blocking collectives, on_device(): lax.psum(jnp.sum(direction * applied, axis=(1, 2)), ('band', 'lon'))  102 us
    dynamic_update_slice x16, other arithmetic, on_device(): lax.map(leaf_blocks, (jnp.transpose(position, (1, 0, 2)), near_rows, near...  45.3 us
    dot_general x2, matrix products, on_device(): jnp.einsum('lspq,mlsq->mlp', near_blocks, rim_values[:, near_rows], preci...  42.9 us
    all_gather x2, blocking collectives, on_device(): band_coeffs = lax.all_gather(panel_coeffs, 'band', axis=1, tiled=True)  38 us
    slice x16, local copies, waits for them, and re-layouts, matern_block(): rows_pos[component][None, :, None] - cols_pos[component][:, None, :]  22 us
    mul x16, local copies, waits for them, and re-layouts, leaf_blocks(): matern_block(rows_pos, cols_pos, length_scale) * slot_mask[:, None, None]  20 us
  transfers between devices with their start and end apart: 6, of which 2 were waited for; matrix products, arithmetic and copies ran while one was open for 20% of the time, Pallas kernels for 0%

commit v1 on v0

--- a/solution.py
+++ b/solution.py
@@ -9,6 +9,11 @@
 HIGHEST_PRECISION = lax.Precision.HIGHEST
 ROOT_THREE = math.sqrt(3.0)
 AMPLITUDE = 0.02
+
+
+def gather_by_exchange(x, axis, dim):
+    copies = jnp.concatenate([x] * lax.axis_size(axis), axis=dim)
+    return lax.all_to_all(copies, axis, dim, dim, tiled=True)
 
 
 def extended(cells, sides, width):
@@ -104,7 +109,7 @@
         )
         upward = jnp.einsum("lab,mla->mlb", transfer, coeffs, precision=HIGHEST_PRECISION)
         panel_coeffs = jnp.einsum("lk,mlb->mkb", membership, upward, precision=HIGHEST_PRECISION)
-        band_coeffs = lax.all_gather(panel_coeffs, "band", axis=1, tiled=True)
+        band_coeffs = gather_by_exchange(panel_coeffs, "band", 1)
         panel_far = jnp.einsum(
             "ksab,mksb->mka",
             panel_couple,

time: 558 us -> 543 us (0.973)
  blocking collectives: 347 us -> 303 us
  other arithmetic: 54.6 us -> 72.2 us
  starting transfers between devices: 16.9 us -> 23.6 us
    all_gather x2 -> x0, blocking collectives: 38 us -> none  [on_device(): band_coeffs = lax.all_gather(panel_coeffs, 'band', axis=1, tiled=True)]
    select_n x16, other arithmetic: 0.12 us -> 11.1 us  [leaf_blocks(): cols_pos = rim_pos[:, rows_index]]
    slice x16, local copies, waits for them, and re-layouts: 22 us -> 12.7 us  [matern_block(): rows_pos[component][None, :, None] - cols_pos[component][:, None, :]]
    all_to_all x0 -> x2, starting transfers between devices: none -> 8.56 us  [gather_by_exchange(): return lax.all_to_all(copies, axis, dim, dim, tiled=True)]
    concatenate x0 -> x4, local copies, waits for them, and re-layouts: none -> 5.63 us  [gather_by_exchange(): copies = jnp.concatenate([x] * lax.axis_size(axis), axis=dim)]
  transfers between devices with their start and end apart: 6 -> 8, of which waited for: 2 -> 1; matrix products, arithmetic and copies ran while one was open for 20% -> 24% of each run, Pallas kernels for 0% -> 0%
where the time goes in v1:
time: 543 us; the launch traced here: 540 us
  blocking collectives  303 us (56%)
  other arithmetic  72.2 us (13%)
  local copies, waits for them, and re-layouts  71.1 us (13%)
  matrix products  64.4 us (12%)
  starting transfers between devices  23.6 us (4%)
    psum x2, blocking collectives, square_total(): return lax.psum(jnp.sum(vector * vector, axis=(1, 2)), ('band', 'lon'))  204 us
    psum x1, blocking collectives, on_device(): lax.psum(jnp.sum(direction * applied, axis=(1, 2)), ('band', 'lon'))  99.5 us
    dynamic_update_slice x16, other arithmetic, on_device(): lax.map(leaf_blocks, (jnp.transpose(position, (1, 0, 2)), near_rows, near...  45 us
    dot_general x2, matrix products, on_device(): jnp.einsum('lspq,mlsq->mlp', near_blocks, rim_values[:, near_rows], preci...  43.1 us
    mul x16, local copies, waits for them, and re-layouts, leaf_blocks(): matern_block(rows_pos, cols_pos, length_scale) * slot_mask[:, None, None]  20.2 us
    slice x16, local copies, waits for them, and re-layouts, matern_block(): rows_pos[component][None, :, None] - cols_pos[component][:, None, :]  12.7 us
    select_n x16, other arithmetic, leaf_blocks(): cols_pos = rim_pos[:, rows_index]  11.1 us
  transfers between devices with their start and end apart: 8, of which 1 were waited for; matrix products, arithmetic and copies ran while one was open for 24% of the time, Pallas kernels for 0%

profile of v1, /device:TPU:1, one launch (start us, length us, event | category | flops | bytes accessed | tf_op | source)
XLA Modules:
  0.0 540.4 jit_solution(11208897973500850381)
XLA Ops:
  1.7 3.0 collective-permute-start.2
  4.7 3.9 collective-permute-start.3
  14.7 4.2 all-to-all-start
  20.5 5.7 %collective-permute-start.1 = (f32[16,6,320]{2,0,1:T(8,128)}, f32[16,6,320]{2,0,1:T(8,128)}, u32[]{:S(2)}, u32[]{:S(2)}) collective-permute-start(f32[16,6,320]{2,0,1:T(8,128)} %get-tuple-element.113), channel_id=1, source_target_pairs={{1,0},{2,1},{3,2},{4,3},{5,4},{6,5},{7,6},{8,7},{9,8},{10,9},{11,1... | collective-permute-start | bytes 368648 | tf_op jit(solution)/shard_map/ppermute | solution.py:28
  31.5 99.0 %while.12 = (s32[]{:T(128)}, f32[16,5,256,256]{3,2,1,0:T(8,128)}, f32[16,3,256]{2,1,0:T(4,128)}, s32[16,5]{1,0:T(8,128)}, f32[3,20,256]{2,0,1:T(4,128)S(1)}, /*i...) while((s32[]{:T(128)}, f32[16,5,256,256]{3,2,1,0:T(8,128)}, f32[16,3,256]{2,1,0:T(4,128)}, ...), condition=%wide.region_3.4_spmd, body=%wide.region_2.3_spmd.sunk | while | flops 4588563 | bytes 1432341 | solution.py:80
  47.2 2.8 multiply_dynamic-update-slice_fusion.2
  53.4 2.8 multiply_dynamic-update-slice_fusion.2
  59.6 2.8 multiply_dynamic-update-slice_fusion.2
  71.9 2.9 multiply_dynamic-update-slice_fusion.2
  78.2 2.8 multiply_dynamic-update-slice_fusion.2
  90.5 2.9 multiply_dynamic-update-slice_fusion.2
  103.0 2.8 multiply_dynamic-update-slice_fusion.2
  115.3 2.8 multiply_dynamic-update-slice_fusion.2
  121.5 2.8 multiply_dynamic-update-slice_fusion.2
  127.7 2.8 multiply_dynamic-update-slice_fusion.2
  143.5 2.9 convolution_bitcast_fusion.9
  150.6 21.6 %fusion.6 = f32[16,16,256]{2,0,1:T(8,128)S(1)} fusion(f32[16,16,5,256]{3,0,2,1:T(8,128)} %bitcast.162, f32[16,5,256,256]{3,2,1,0:T(8,128)} %get-tuple-element.79, f32[16,256]{1,0:T(8,128)S(1)} %copy-done.22, f32[16,16,256]{2,1,0:T(8,128)S(1)} %copy-done.1), kind=kOutput, calls=%fused_computation.28 | convolution fusion | flops 1006764032 | bytes 22822912 | tf_op jit(solution)/shard_map/lspq,mlsq->mlp/dot_general | solution.py:104
  173.1 104.8 %all-reduce = (f32[16]{0:T(128)S(1)}, f32[16]{0:T(128)S(1)}) all-reduce(f32[16]{0:T(128)S(1)} %copy-done.29, f32[16]{0:T(128)S(1)} %get-tuple-element.120), channel_id=1, replica_groups=mesh['band'=16,'lon'=32] {'band','lon'}, use_global_device_ids=true, to_apply=%region_1.2 | all-reduce | flops 32 | bytes 256 | tf_op jit(solution)/shard_map/psum | solution.py:90
  278.2 99.1 %psum.30 = f32[16]{0:T(128)S(1)} all-reduce(f32[16]{0:T(128)S(1)} %multiply_reduce_fusion.1), channel_id=1, replica_groups=mesh['band'=16,'lon'=32] {'band','lon'}, use_global_device_ids=true, to_apply=%region_7.8 | all-reduce | flops 16 | bytes 128 | tf_op jit(solution)/shard_map/psum | solution.py:90
  386.9 4.4 all-to-all-start.1
  393.7 4.2 all-to-all-done.1
  409.6 3.5 convolution_bitcast_fusion.6
  415.8 21.5 %fusion.5 = f32[16,16,256]{2,0,1:T(8,128)S(1)} fusion(f32[16,16,5,256]{3,0,2,1:T(8,128)} %bitcast.161, f32[16,5,256,256]{3,2,1,0:T(8,128)} %get-tuple-element.79, f32[16,16,256]{2,0,1:T(8,128)S(1)} %multiply_add_fusion.1, f32[16,256]{1,0:T(8,128)S(1)} %copy-done.22), kind=kOutput, calls=%fused_computation.26 | convolution fusion | flops 1006764032 | bytes 22822912 | tf_op jit(solution)/shard_map/lspq,mlsq->mlp/dot_general | solution.py:104
  439.0 99.5 %psum.31 = f32[16]{0:T(128)S(1)} all-reduce(f32[16]{0:T(128)S(1)} %get-tuple-element.122), channel_id=1, replica_groups=mesh['band'=16,'lon'=32] {'band','lon'}, use_global_device_ids=true, to_apply=%region_9.10 | all-reduce | flops 16 | bytes 128 | tf_op jit(solution)/shard_map/psum | solution.py:125
  (268 shorter events, 132.3 us)
Async XLA Ops:
  0.6 142.9 %copy-start = (f32[16,4,64,64]{3,2,1,0:T(8,128)S(1)}, f32[16,4,64,64]{3,2,1,0:T(8,128)}, u32[]{:S(2)}) copy-start(f32[16,4,64,64]{3,2,1,0:T(8,128)} %param.17) | copy-start | bytes 3145732
  0.7 10.9 %copy-start.23 = (s32[16]{0:T(128)S(1)}, s32[16]{0:T(128)}, u32[]{:S(2)}) copy-start(s32[16]{0:T(128)} %param.23) | copy-start | bytes 196
  1.7 28.3 %collective-permute-start.2 = (f32[3,2,256]{2,0,1:T(4,128)S(1)}, f32[3,2,256]{2,0,1:T(4,128)S(1)}, u32[]{:S(2)}, u32[]{:S(2)}) collective-permute-start(f32[3,2,256]{2,0,1:T(4,128)S(1)} %get-tuple-element.116), channel_id=1, source_target_pairs={{0,1},{1,2},{2,3},{3,4},{4,5},{5,6},{6,7},{7,8},{8,9},{9,10},{10,1... | collective-permute-start | bytes 18440 | tf_op jit(solution)/shard_map/ppermute | solution.py:26
  4.7 25.9 %collective-permute-start.3 = (f32[3,2,256]{2,0,1:T(4,128)S(1)}, f32[3,2,256]{2,0,1:T(4,128)}, u32[]{:S(2)}, u32[]{:S(2)}) collective-permute-start(f32[3,2,256]{2,0,1:T(4,128)S(1)} %get-tuple-element.117), channel_id=1, source_target_pairs={{1,0},{2,1},{3,2},{4,3},{5,4},{6,5},{7,6},{8,7},{9,8},{10,9},{11,1... | collective-permute-start | bytes 18440 | tf_op jit(solution)/shard_map/ppermute | solution.py:28
  11.0 128.6 %copy-start.7 = (f32[16,16,64]{2,0,1:T(8,128)}, f32[16,16,64]{2,0,1:T(8,128)S(1)}, u32[]{:S(2)}) copy-start(f32[16,16,64]{2,0,1:T(8,128)S(1)} %convolution_bitcast_fusion.11) | copy-start | bytes 196612
  12.0 15.0 %copy-start.26 = (s32[16,5]{0,1:T(8,128)S(1)}, s32[16,5]{0,1:T(8,128)}, u32[]{:S(2)}) copy-start(s32[16,5]{0,1:T(8,128)} %param.20) | copy-start | bytes 964
  12.0 15.1 %copy-start.28 = (s32[2,2]{1,0:T(2,128)S(1)}, s32[2,2]{1,0:T(2,128)}, u32[]{:S(2)}) copy-start(s32[2,2]{1,0:T(2,128)} %param.22) | copy-start | bytes 52
  12.0 15.8 %copy-start.27 = (s32[16,4]{0,1:T(4,128)S(1)}, s32[16,4]{0,1:T(4,128)}, u32[]{:S(2)}) copy-start(s32[16,4]{0,1:T(4,128)} %param.21) | copy-start | bytes 772
  14.7 115.9 %all-to-all-start = ((f32[16,1,2048]{2,1,0:T(1,128)}), f32[16,1,2048]{2,1,0:T(1,128)}, u32[]{:S(2)}, u32[]{:S(2)}) async-start(f32[16,1,2048]{2,1,0:T(1,128)} %reshape.181), calls=%async_computation | async-start | bytes 262144 | tf_op jit(solution)/shard_map/all_to_all | solution.py:16
  19.8 119.8 %collective-permute-start = (f32[16,6,320]{2,0,1:T(8,128)}, f32[16,6,320]{2,0,1:T(8,128)S(1)}, u32[]{:S(2)}, u32[]{:S(2)}) collective-permute-start(f32[16,6,320]{2,0,1:T(8,128)} %get-tuple-element.112), channel_id=1, source_target_pairs={{0,1},{1,2},{2,3},{3,4},{4,5},{5,6},{6,7},{7,8},{8,9},{9,10},{10,1... | collective-permute-start | bytes 368648 | tf_op jit(solution)/shard_map/ppermute | solution.py:26
  20.5 119.0 %collective-permute-start.1 = (f32[16,6,320]{2,0,1:T(8,128)}, f32[16,6,320]{2,0,1:T(8,128)}, u32[]{:S(2)}, u32[]{:S(2)}) collective-permute-start(f32[16,6,320]{2,0,1:T(8,128)} %get-tuple-element.113), channel_id=1, source_target_pairs={{1,0},{2,1},{3,2},{4,3},{5,4},{6,5},{7,6},{8,7},{9,8},{10,9},{11,1... | collective-permute-start | bytes 368648 | tf_op jit(solution)/shard_map/ppermute | solution.py:28
  28.0 113.1 %copy-start.19 = (s32[1024]{0:T(1024)}, s32[1024]{0:T(1024)S(1)}, u32[]{:S(2)}) copy-start(s32[1024]{0:T(1024)S(1)} %pad_clamp_fusion.2) | copy-start | bytes 12292
  150.6 21.6 %copy-start.2 = (f32[16,256,64]{1,2,0:T(8,128)S(1)}, f32[16,256,64]{1,2,0:T(8,128)}, u32[]{:S(2)}) copy-start(f32[16,256,64]{1,2,0:T(8,128)} %param.16) | copy-start | bytes 3145732
  150.6 21.7 %copy-start.14 = (f32[16,16,64]{2,0,1:T(8,128)S(1)}, f32[16,16,64]{2,0,1:T(8,128)}, u32[]{:S(2)}) copy-start(f32[16,16,64]{2,0,1:T(8,128)} %fusion.8) | copy-start | bytes 196612
  173.1 206.6 %copy-start.5 = (f32[16,16,256]{2,0,1:T(8,128)}, f32[16,16,256]{2,0,1:T(8,128)S(1)}, u32[]{:S(2)}) copy-start(f32[16,16,256]{2,0,1:T(8,128)S(1)} %get-tuple-element.121) | copy-start | bytes 786436
  380.6 10.7 %copy-start.10 = (f32[16,16,64]{2,0,1:T(8,128)S(1)}, f32[16,16,64]{2,0,1:T(8,128)}, u32[]{:S(2)}) copy-start(f32[16,16,64]{2,0,1:T(8,128)} %copy-done.9) | copy-start | bytes 196612
  386.9 11.0 %all-to-all-start.1 = ((f32[16,1,2048]{2,1,0:T(1,128)}), f32[16,1,2048]{2,1,0:T(1,128)}, u32[]{:S(2)}, u32[]{:S(2)}) async-start(f32[16,1,2048]{2,1,0:T(1,128)} %reshape.183), calls=%async_computation.1 | async-start | bytes 262144 | tf_op jit(solution)/shard_map/all_to_all | solution.py:16
  391.3 16.0 %copy-start.20 = (s32[1024]{0:T(1024)S(1)}, s32[1024]{0:T(1024)}, u32[]{:S(2)}) copy-start(s32[1024]{0:T(1024)} %copy-done.19) | copy-start | bytes 12292
  392.1 13.7 %collective-permute-start.4 = (f32[16,6,320]{2,0,1:T(8,128)}, f32[16,6,320]{2,0,1:T(8,128)S(1)}, u32[]{:S(2)}, u32[]{:S(2)}) collective-permute-start(f32[16,6,320]{2,0,1:T(8,128)} %get-tuple-element.110), channel_id=1, source_target_pairs={{0,1},{1,2},{2,3},{3,4},{4,5},{5,6},{6,7},{7,8},{8,9},{9,10},{10,1... | collective-permute-start | bytes 368648 | tf_op jit(solution)/shard_map/ppermute | solution.py:26
  393.7 12.1 %collective-permute-start.5 = (f32[16,6,320]{2,0,1:T(8,128)}, f32[16,6,320]{2,0,1:T(8,128)}, u32[]{:S(2)}, u32[]{:S(2)}) collective-permute-start(f32[16,6,320]{2,0,1:T(8,128)} %get-tuple-element.111), channel_id=1, source_target_pairs={{1,0},{2,1},{3,2},{4,3},{5,4},{6,5},{7,6},{8,7},{9,8},{10,9},{11,1... | collective-permute-start | bytes 368648 | tf_op jit(solution)/shard_map/ppermute | solution.py:28
  415.8 21.5 %copy-start.15 = (f32[16,16,64]{2,1,0:T(8,128)S(1)}, f32[16,16,64]{2,1,0:T(8,128)}, u32[]{:S(2)}) copy-start(f32[16,16,64]{2,1,0:T(8,128)} %convolution_bitcast_fusion.4) | copy-start | bytes 196612
  415.8 21.5 %copy-start.17 = (f32[16,16,64]{2,1,0:T(8,128)S(1)}, f32[16,16,64]{2,1,0:T(8,128)}, u32[]{:S(2)}) copy-start(f32[16,16,64]{2,1,0:T(8,128)} %convolution_bitcast_fusion.6) | copy-start | bytes 196612
  415.8 22.4 %copy-start.3 = (f32[16,256,64]{1,2,0:T(8,128)S(1)}, f32[16,256,64]{1,2,0:T(8,128)}, u32[]{:S(2)}) copy-start(f32[16,256,64]{1,2,0:T(8,128)} %param.16) | copy-start | bytes 3145732
  437.3 101.2 %copy-start.6 = (f32[16,16,256]{2,0,1:T(8,128)S(1)}, f32[16,16,256]{2,0,1:T(8,128)}, u32[]{:S(2)}) copy-start(f32[16,16,256]{2,0,1:T(8,128)} %copy-done.5) | copy-start | bytes 786436
  (14 other events, 55.9 us)
